TPU v7x, 256 devices: a whole 4x4x8 slice. The times are simulated.
256 devices in a mesh: section: 8 (over x, core), expert: 32 (over z, y).
Axes of the slice: x: 4, y: 4, z: 8, core: 2. Of those that a mesh axis runs over, the one named last changes fastest.
Arguments:
- tokens: bfloat16 [8, 2304, 2048], P(None, 'expert'), may hold values from -6 to 6
- w_in: bfloat16 [8, 2048, 2048], P('section', 'expert'), may hold values from -0.125 to 0.125
- w_out: bfloat16 [8, 2048, 2048], P('section', 'expert'), may hold values from -0.125 to 0.125
- router: bfloat16 [2048, 32], replicated, may hold values from -0.125 to 0.125
- exp_in: bfloat16 [32, 2048, 2048], P('expert', None, 'section'), may hold values from -0.125 to 0.125
- exp_out: bfloat16 [32, 2048, 2048], P('expert', 'section'), may hold values from -0.375 to 0.375
- active_rows: int32 [4608], P('expert'), may hold values from 0 to 575, as said below
- active_expert: int32 [4608, 1], P('expert'), may hold values from 0 to 31; in each aligned block of 144 rows (0 to 143, 144 to 287, ...) at most 13 rows name the same one
Outputs:
- updated: bfloat16 [8, 2304, 2048], P(None, 'expert', 'section')
Inputs may be any that keep to these rules, and one draw needn't show every extreme that they name: `active_rows`: the 144 entries of one token block name distinct rows of its 576 rows. `active_expert`: among the 144 entries of one token block no expert is named more than 13 times.
All inputs are finite; a program needn't handle non-finite values.
Results may differ from a plain program's by a relative error of at most 0.024.
Values may be sent and summed in bfloat16 or wider, within the bound.
No kernel may reach another device: no remote copies, remote signals or barrier semaphores. Data moves between devices by JAX's collectives and lax.ppermute only.
A program may use at most 64 MiB of HBM per device.

v0:
```python
import jax
import jax.numpy as jnp
from jax import lax
from jax.sharding import PartitionSpec as P


def from_behind(value, axis, steps):
    count = lax.axis_size(axis)
    initial, last = (max(0, -steps), min(count, count - steps))
    return lax.ppermute(value, axis, [(source, source + steps) for source in range(initial, last)])


def normalize(rows):
    wide = rows.astype(jnp.float32)
    scale = lax.rsqrt(jnp.mean(wide * wide, axis=-1, keepdims=True) + 1e-05)
    return wide * scale


def processor(stream, w_first, w_second):
    normed = normalize(stream).astype(jnp.bfloat16)
    hidden = jax.nn.silu(jnp.dot(normed, w_first, preferred_element_type=jnp.float32)).astype(
        jnp.bfloat16
    )
    branch = jnp.dot(hidden, w_second, preferred_element_type=jnp.float32)
    return (stream.astype(jnp.float32) + branch).astype(jnp.bfloat16)


def local(tokens, w_in, w_out, router, exp_in, exp_out, active_rows, active_expert):
    n_section = lax.axis_size("section")
    n_expert = lax.axis_size("expert")
    section = lax.axis_index("section")
    expert_index = lax.axis_index("expert")
    micro, tok_dev, width = tokens.shape
    w_first, w_second = (
        lax.all_gather(w_in, "expert", axis=1, tiled=True),
        lax.all_gather(w_out, "expert", axis=1, tiled=True),
    )
    w_first = w_first[0]
    w_second = w_second[0]
    last = n_section - 1

    def run_layer(stream):
        return processor(stream, w_first, w_second)

    def skip_layer(stream):
        return jnp.zeros_like(stream)

    def tick(step, carry):
        incoming, collected = carry
        micro_index = step - section
        valid = (micro_index >= 0) & (micro_index < micro)
        clamped = jnp.clip(micro_index, 0, micro - 1)
        fresh = lax.dynamic_index_in_dim(tokens, clamped, 0, keepdims=False)
        stream = jnp.where(section == 0, fresh, incoming)
        result = lax.cond(valid, run_layer, skip_layer, stream)
        updated = lax.dynamic_update_index_in_dim(collected, result, clamped, 0)
        collected = jnp.where(valid & (section == last), updated, collected)
        passed = from_behind(result, "section", 1)
        return (passed, collected)

    start = (jnp.zeros((tok_dev, width), jnp.bfloat16), jnp.zeros_like(tokens))
    passed, collected = lax.fori_loop(0, micro + n_section - 1, tick, start)
    rows_dev = micro * tok_dev
    flat = collected.reshape(rows_dev, width)
    n_exp = router.shape[1]
    part_width = width // n_section
    per_sub = 2
    ranks = n_section * per_sub
    chosen = active_expert[:, 0]
    onehot = chosen[:, None] == jnp.arange(n_exp, dtype=jnp.int32)[None, :]
    counts = onehot.astype(jnp.int32)
    earlier = jnp.cumsum(counts, axis=0) - counts
    rank = jnp.sum(earlier * counts, axis=1)
    picked = jnp.take(flat, active_rows, axis=0)
    contact = normalize(picked).astype(jnp.bfloat16)
    share = rank // per_sub
    slot = (share * n_exp + chosen) * per_sub + rank % per_sub
    placing = (
        jnp.arange(n_section * n_exp * per_sub, dtype=jnp.int32)[:, None] == slot[None, :]
    ).astype(jnp.bfloat16)
    dispatch = jnp.dot(placing, contact, preferred_element_type=jnp.float32).astype(jnp.bfloat16)
    dispatch = dispatch.reshape(n_section, n_exp * per_sub, width)
    columns = flat.reshape(rows_dev, n_section, part_width).transpose(1, 0, 2)
    columns = columns.reshape(n_section, rows_dev * part_width // width, width)
    payload = jnp.concatenate([columns, dispatch], axis=1)
    mine = payload[last]
    for target in range(n_section - 1):
        got = lax.ppermute(payload[target], "section", [(last, target)])
        mine = jnp.where(section == target, got, mine)
    base_rows = rows_dev * part_width // width
    base = mine[:base_rows].reshape(rows_dev, part_width)
    outgoing = mine[base_rows:].reshape(n_exp, per_sub, width)
    arrived = lax.all_to_all(outgoing, "expert", split_axis=0, concat_axis=0, tiled=True)
    rows = lax.all_gather(arrived, "section", axis=0, tiled=True).reshape(-1, width)
    e_first = exp_in[0]
    e_second = exp_out[0]
    column = lax.dynamic_slice_in_dim(router, expert_index, 1, 1)
    logits = jnp.dot(rows, column, preferred_element_type=jnp.float32)[:, 0]
    gate = jax.nn.sigmoid(logits)
    hidden = jax.nn.silu(jnp.dot(rows, e_first, preferred_element_type=jnp.float32)).astype(
        jnp.bfloat16
    )
    partial_value = jnp.dot(hidden, e_second, preferred_element_type=jnp.float32)
    scaled = (gate[:, None] * partial_value).astype(jnp.bfloat16)
    summed = lax.psum_scatter(scaled, "section", scatter_dimension=1, tiled=True)
    summed = summed.reshape(n_section, n_expert, per_sub, part_width).transpose(1, 0, 2, 3)
    returned = lax.all_to_all(summed, "expert", split_axis=0, concat_axis=0, tiled=True)
    returned = returned.reshape(n_exp * ranks, part_width)
    position = chosen * ranks + rank
    added = jnp.take(returned, position, axis=0).astype(jnp.float32)
    mixed = base.astype(jnp.float32).at[active_rows].add(added)
    return mixed.astype(jnp.bfloat16).reshape(micro, tok_dev, part_width)


def solution(mesh):
    return jax.shard_map(
        local,
        mesh=mesh,
        in_specs=(
            P(None, "expert", None),
            P("section", "expert", None),
            P("section", "expert", None),
            P(),
            P("expert", None, "section"),
            P("expert", "section", None),
            P("expert"),
            P("expert", None),
        ),
        out_specs=P(None, "expert", "section"),
        check_vma=False,
    )
```

profile of v0, /device:TPU:7, one launch (start us, length us, event | category | flops | bytes accessed | tf_op | source)
XLA Modules:
  0.0 662.8 jit_solution(12632711766562289976)
XLA Ops:
  12.4 97.6 %all-gather.4.cloned.1.call-done = bf16[1,2048,2048]{2,1,0:T(8,128)(2,1)} async-done(((bf16[1,64,2048]{2,1,0:T(8,128)(2,1)}), bf16[1,2048,2048]{2,1,0:T(8,128)(2,1)}) %all-gather.4.cloned.1.call-update) | async-done | bytes 8388624 | tf_op jit(solution)/shard_map/all_gather | solution.py:35
  110.0 97.6 %all-gather.6.cloned.1.call-done = bf16[1,2048,2048]{2,1,0:T(8,128)(2,1)} async-done(((bf16[1,64,2048]{2,1,0:T(8,128)(2,1)}), bf16[1,2048,2048]{2,1,0:T(8,128)(2,1)}) %all-gather.6.cloned.1.call-update) | async-done | bytes 8388624 | tf_op jit(solution)/shard_map/all_gather | solution.py:36
  208.6 290.4 %while.16 = (s32[]{:T(128)}, bf16[72,2048]{1,0:T(8,128)(2,1)}, bf16[8,72,2048]{2,1,0:T(8,128)(2,1)S(1)}, s32[]{:T(128)}, pred[]{:T(512)}, /*index=5*/bf16[8,72,2...) while((s32[]{:T(128)}, bf16[72,2048]{1,0:T(8,128)(2,1)}, ...), condition=%wide.region_4.5_spmd, body=%wide.region_0.4_spmd.sunk | while | flops 1210613888 | bytes 21499308 | solution.py:62
  211.5 3.3 collective-permute-done
  217.7 6.9 %collective-permute-done = bf16[72,2048]{1,0:T(8,128)(2,1)} collective-permute-done((bf16[72,2048]{1,0:T(8,128)(2,1)}, bf16[72,2048]{1,0:T(8,128)(2,1)}, u32[]{:S(2)}, u32[]{:S(2)}) %collective-permute-start) | collective-permute-done | bytes 294944 | tf_op jit(solution)/shard_map/while/body/eval_jaxpr/ppermute | solution.py:10
  224.6 1.5 conditional.2
  227.5 6.9 %collective-permute-done = bf16[72,2048]{1,0:T(8,128)(2,1)} collective-permute-done((bf16[72,2048]{1,0:T(8,128)(2,1)}, bf16[72,2048]{1,0:T(8,128)(2,1)}, u32[]{:S(2)}, u32[]{:S(2)}) %collective-permute-start) | collective-permute-done | bytes 294944 | tf_op jit(solution)/shard_map/while/body/eval_jaxpr/ppermute | solution.py:10
  237.4 6.9 %collective-permute-done = bf16[72,2048]{1,0:T(8,128)(2,1)} collective-permute-done((bf16[72,2048]{1,0:T(8,128)(2,1)}, bf16[72,2048]{1,0:T(8,128)(2,1)}, u32[]{:S(2)}, u32[]{:S(2)}) %collective-permute-start) | collective-permute-done | bytes 294944 | tf_op jit(solution)/shard_map/while/body/eval_jaxpr/ppermute | solution.py:10
  247.2 6.9 %collective-permute-done = bf16[72,2048]{1,0:T(8,128)(2,1)} collective-permute-done((bf16[72,2048]{1,0:T(8,128)(2,1)}, bf16[72,2048]{1,0:T(8,128)(2,1)}, u32[]{:S(2)}, u32[]{:S(2)}) %collective-permute-start) | collective-permute-done | bytes 294944 | tf_op jit(solution)/shard_map/while/body/eval_jaxpr/ppermute | solution.py:10
  257.0 6.9 %collective-permute-done = bf16[72,2048]{1,0:T(8,128)(2,1)} collective-permute-done((bf16[72,2048]{1,0:T(8,128)(2,1)}, bf16[72,2048]{1,0:T(8,128)(2,1)}, u32[]{:S(2)}, u32[]{:S(2)}) %collective-permute-start) | collective-permute-done | bytes 294944 | tf_op jit(solution)/shard_map/while/body/eval_jaxpr/ppermute | solution.py:10
  266.8 67.4 %collective-permute-done = bf16[72,2048]{1,0:T(8,128)(2,1)} collective-permute-done((bf16[72,2048]{1,0:T(8,128)(2,1)}, bf16[72,2048]{1,0:T(8,128)(2,1)}, u32[]{:S(2)}, u32[]{:S(2)}) %collective-permute-start) | collective-permute-done | bytes 294944 | tf_op jit(solution)/shard_map/while/body/eval_jaxpr/ppermute | solution.py:10
  334.3 12.8 %conditional.2 = (bf16[72,2048]{1,0:T(8,128)(2,1)}, bf16[1,72,2048]{2,1,0:T(8,128)(2,1)}) conditional(s32[]{:T(128)} %convert_element_type.108, () %tuple.53, (pred[]{:T(512)}, bf16[8,72,2048]{2,1,0:T(8,128)(2,1)}, s32[]{:T(128)}, bf16[72,2048]{1,0:T(8,128)(2,1)}, bf16[2048,2048]{1,0:T(8,128)(2,1)}, /*index=5*/bf16[2048,2048]{1,0:T(8,128)(2,1)}) %tuple.54), branch_computations={%region_1.1_spmd, %region_2.3_spmd} | conditional | flops 1210466432 | bytes 19434644 | solution.py:55
  335.6 9.8 %fusion = bf16[72,2048]{1,0:T(8,128)(2,1)} fusion(bf16[2048,2048]{1,0:T(8,128)(2,1)} %get-tuple-element.195, bf16[2048,2048]{1,0:T(8,128)(2,1)} %get-tuple-element.194, f32[72]{0:T(128)S(1)} %add_rsqrt_fusion, bf16[72,2048]{1,0:T(8,128)(2,1)} %get-tuple-element.193, bf16[8,72,2048]{2,1,0:T(8,128)(2,1)} %get-tuple-element.191, s32[]{:T(128)} %get-tuple-element.192, ...), kind=kOutput, calls=%fused_computation.4 | convolution fusion | flops 1209876480 | bytes 18254112 | tf_op jit(solution)/shard_map/while/body/eval_jaxpr/cond/branch_1_fun/dot_general | solution.py:24
  345.4 1.7 copy.30
  349.5 6.0 collective-permute-done
  355.4 12.8 %conditional.2 = (bf16[72,2048]{1,0:T(8,128)(2,1)}, bf16[1,72,2048]{2,1,0:T(8,128)(2,1)}) conditional(s32[]{:T(128)} %convert_element_type.108, () %tuple.53, (pred[]{:T(512)}, bf16[8,72,2048]{2,1,0:T(8,128)(2,1)}, s32[]{:T(128)}, bf16[72,2048]{1,0:T(8,128)(2,1)}, bf16[2048,2048]{1,0:T(8,128)(2,1)}, /*index=5*/bf16[2048,2048]{1,0:T(8,128)(2,1)}) %tuple.54), branch_computations={%region_1.1_spmd, %region_2.3_spmd} | conditional | flops 1210466432 | bytes 19434644 | solution.py:55
  356.7 9.8 %fusion = bf16[72,2048]{1,0:T(8,128)(2,1)} fusion(bf16[2048,2048]{1,0:T(8,128)(2,1)} %get-tuple-element.195, bf16[2048,2048]{1,0:T(8,128)(2,1)} %get-tuple-element.194, f32[72]{0:T(128)S(1)} %add_rsqrt_fusion, bf16[72,2048]{1,0:T(8,128)(2,1)} %get-tuple-element.193, bf16[8,72,2048]{2,1,0:T(8,128)(2,1)} %get-tuple-element.191, s32[]{:T(128)} %get-tuple-element.192, ...), kind=kOutput, calls=%fused_computation.4 | convolution fusion | flops 1209876480 | bytes 18254112 | tf_op jit(solution)/shard_map/while/body/eval_jaxpr/cond/branch_1_fun/dot_general | solution.py:24
  366.6 1.7 copy.30
  370.6 6.0 collective-permute-done
  376.6 12.8 %conditional.2 = (bf16[72,2048]{1,0:T(8,128)(2,1)}, bf16[1,72,2048]{2,1,0:T(8,128)(2,1)}) conditional(s32[]{:T(128)} %convert_element_type.108, () %tuple.53, (pred[]{:T(512)}, bf16[8,72,2048]{2,1,0:T(8,128)(2,1)}, s32[]{:T(128)}, bf16[72,2048]{1,0:T(8,128)(2,1)}, bf16[2048,2048]{1,0:T(8,128)(2,1)}, /*index=5*/bf16[2048,2048]{1,0:T(8,128)(2,1)}) %tuple.54), branch_computations={%region_1.1_spmd, %region_2.3_spmd} | conditional | flops 1210466432 | bytes 19434644 | solution.py:55
  377.9 9.8 %fusion = bf16[72,2048]{1,0:T(8,128)(2,1)} fusion(bf16[2048,2048]{1,0:T(8,128)(2,1)} %get-tuple-element.195, bf16[2048,2048]{1,0:T(8,128)(2,1)} %get-tuple-element.194, f32[72]{0:T(128)S(1)} %add_rsqrt_fusion, bf16[72,2048]{1,0:T(8,128)(2,1)} %get-tuple-element.193, bf16[8,72,2048]{2,1,0:T(8,128)(2,1)} %get-tuple-element.191, s32[]{:T(128)} %get-tuple-element.192, ...), kind=kOutput, calls=%fused_computation.4 | convolution fusion | flops 1209876480 | bytes 18254112 | tf_op jit(solution)/shard_map/while/body/eval_jaxpr/cond/branch_1_fun/dot_general | solution.py:24
  387.7 1.7 copy.30
  391.8 6.0 collective-permute-done
  397.8 12.8 %conditional.2 = (bf16[72,2048]{1,0:T(8,128)(2,1)}, bf16[1,72,2048]{2,1,0:T(8,128)(2,1)}) conditional(s32[]{:T(128)} %convert_element_type.108, () %tuple.53, (pred[]{:T(512)}, bf16[8,72,2048]{2,1,0:T(8,128)(2,1)}, s32[]{:T(128)}, bf16[72,2048]{1,0:T(8,128)(2,1)}, bf16[2048,2048]{1,0:T(8,128)(2,1)}, /*index=5*/bf16[2048,2048]{1,0:T(8,128)(2,1)}) %tuple.54), branch_computations={%region_1.1_spmd, %region_2.3_spmd} | conditional | flops 1210466432 | bytes 19434644 | solution.py:55
  399.0 9.8 %fusion = bf16[72,2048]{1,0:T(8,128)(2,1)} fusion(bf16[2048,2048]{1,0:T(8,128)(2,1)} %get-tuple-element.195, bf16[2048,2048]{1,0:T(8,128)(2,1)} %get-tuple-element.194, f32[72]{0:T(128)S(1)} %add_rsqrt_fusion, bf16[72,2048]{1,0:T(8,128)(2,1)} %get-tuple-element.193, bf16[8,72,2048]{2,1,0:T(8,128)(2,1)} %get-tuple-element.191, s32[]{:T(128)} %get-tuple-element.192, ...), kind=kOutput, calls=%fused_computation.4 | convolution fusion | flops 1209876480 | bytes 18254112 | tf_op jit(solution)/shard_map/while/body/eval_jaxpr/cond/branch_1_fun/dot_general | solution.py:24
  408.9 1.7 copy.30
  412.9 6.0 collective-permute-done
  418.9 12.8 %conditional.2 = (bf16[72,2048]{1,0:T(8,128)(2,1)}, bf16[1,72,2048]{2,1,0:T(8,128)(2,1)}) conditional(s32[]{:T(128)} %convert_element_type.108, () %tuple.53, (pred[]{:T(512)}, bf16[8,72,2048]{2,1,0:T(8,128)(2,1)}, s32[]{:T(128)}, bf16[72,2048]{1,0:T(8,128)(2,1)}, bf16[2048,2048]{1,0:T(8,128)(2,1)}, /*index=5*/bf16[2048,2048]{1,0:T(8,128)(2,1)}) %tuple.54), branch_computations={%region_1.1_spmd, %region_2.3_spmd} | conditional | flops 1210466432 | bytes 19434644 | solution.py:55
  420.2 9.8 %fusion = bf16[72,2048]{1,0:T(8,128)(2,1)} fusion(bf16[2048,2048]{1,0:T(8,128)(2,1)} %get-tuple-element.195, bf16[2048,2048]{1,0:T(8,128)(2,1)} %get-tuple-element.194, f32[72]{0:T(128)S(1)} %add_rsqrt_fusion, bf16[72,2048]{1,0:T(8,128)(2,1)} %get-tuple-element.193, bf16[8,72,2048]{2,1,0:T(8,128)(2,1)} %get-tuple-element.191, s32[]{:T(128)} %get-tuple-element.192, ...), kind=kOutput, calls=%fused_computation.4 | convolution fusion | flops 1209876480 | bytes 18254112 | tf_op jit(solution)/shard_map/while/body/eval_jaxpr/cond/branch_1_fun/dot_general | solution.py:24
  430.0 1.7 copy.30
  434.1 6.0 collective-permute-done
  440.1 12.8 %conditional.2 = (bf16[72,2048]{1,0:T(8,128)(2,1)}, bf16[1,72,2048]{2,1,0:T(8,128)(2,1)}) conditional(s32[]{:T(128)} %convert_element_type.108, () %tuple.53, (pred[]{:T(512)}, bf16[8,72,2048]{2,1,0:T(8,128)(2,1)}, s32[]{:T(128)}, bf16[72,2048]{1,0:T(8,128)(2,1)}, bf16[2048,2048]{1,0:T(8,128)(2,1)}, /*index=5*/bf16[2048,2048]{1,0:T(8,128)(2,1)}) %tuple.54), branch_computations={%region_1.1_spmd, %region_2.3_spmd} | conditional | flops 1210466432 | bytes 19434644 | solution.py:55
  441.3 9.8 %fusion = bf16[72,2048]{1,0:T(8,128)(2,1)} fusion(bf16[2048,2048]{1,0:T(8,128)(2,1)} %get-tuple-element.195, bf16[2048,2048]{1,0:T(8,128)(2,1)} %get-tuple-element.194, f32[72]{0:T(128)S(1)} %add_rsqrt_fusion, bf16[72,2048]{1,0:T(8,128)(2,1)} %get-tuple-element.193, bf16[8,72,2048]{2,1,0:T(8,128)(2,1)} %get-tuple-element.191, s32[]{:T(128)} %get-tuple-element.192, ...), kind=kOutput, calls=%fused_computation.4 | convolution fusion | flops 1209876480 | bytes 18254112 | tf_op jit(solution)/shard_map/while/body/eval_jaxpr/cond/branch_1_fun/dot_general | solution.py:24
  451.2 1.7 copy.30
  455.2 6.0 collective-permute-done
  461.2 12.8 %conditional.2 = (bf16[72,2048]{1,0:T(8,128)(2,1)}, bf16[1,72,2048]{2,1,0:T(8,128)(2,1)}) conditional(s32[]{:T(128)} %convert_element_type.108, () %tuple.53, (pred[]{:T(512)}, bf16[8,72,2048]{2,1,0:T(8,128)(2,1)}, s32[]{:T(128)}, bf16[72,2048]{1,0:T(8,128)(2,1)}, bf16[2048,2048]{1,0:T(8,128)(2,1)}, /*index=5*/bf16[2048,2048]{1,0:T(8,128)(2,1)}) %tuple.54), branch_computations={%region_1.1_spmd, %region_2.3_spmd} | conditional | flops 1210466432 | bytes 19434644 | solution.py:55
  462.5 9.8 %fusion = bf16[72,2048]{1,0:T(8,128)(2,1)} fusion(bf16[2048,2048]{1,0:T(8,128)(2,1)} %get-tuple-element.195, bf16[2048,2048]{1,0:T(8,128)(2,1)} %get-tuple-element.194, f32[72]{0:T(128)S(1)} %add_rsqrt_fusion, bf16[72,2048]{1,0:T(8,128)(2,1)} %get-tuple-element.193, bf16[8,72,2048]{2,1,0:T(8,128)(2,1)} %get-tuple-element.191, s32[]{:T(128)} %get-tuple-element.192, ...), kind=kOutput, calls=%fused_computation.4 | convolution fusion | flops 1209876480 | bytes 18254112 | tf_op jit(solution)/shard_map/while/body/eval_jaxpr/cond/branch_1_fun/dot_general | solution.py:24
  472.4 1.7 copy.30
  476.4 6.0 collective-permute-done
  482.4 12.8 %conditional.2 = (bf16[72,2048]{1,0:T(8,128)(2,1)}, bf16[1,72,2048]{2,1,0:T(8,128)(2,1)}) conditional(s32[]{:T(128)} %convert_element_type.108, () %tuple.53, (pred[]{:T(512)}, bf16[8,72,2048]{2,1,0:T(8,128)(2,1)}, s32[]{:T(128)}, bf16[72,2048]{1,0:T(8,128)(2,1)}, bf16[2048,2048]{1,0:T(8,128)(2,1)}, /*index=5*/bf16[2048,2048]{1,0:T(8,128)(2,1)}) %tuple.54), branch_computations={%region_1.1_spmd, %region_2.3_spmd} | conditional | flops 1210466432 | bytes 19434644 | solution.py:55
  483.7 9.8 %fusion = bf16[72,2048]{1,0:T(8,128)(2,1)} fusion(bf16[2048,2048]{1,0:T(8,128)(2,1)} %get-tuple-element.195, bf16[2048,2048]{1,0:T(8,128)(2,1)} %get-tuple-element.194, f32[72]{0:T(128)S(1)} %add_rsqrt_fusion, bf16[72,2048]{1,0:T(8,128)(2,1)} %get-tuple-element.193, bf16[8,72,2048]{2,1,0:T(8,128)(2,1)} %get-tuple-element.191, s32[]{:T(128)} %get-tuple-element.192, ...), kind=kOutput, calls=%fused_computation.4 | convolution fusion | flops 1209876480 | bytes 18254112 | tf_op jit(solution)/shard_map/while/body/eval_jaxpr/cond/branch_1_fun/dot_general | solution.py:24
  493.5 1.7 copy.30
  499.0 1.8 gather_fusion
  503.0 1.9 copy.25
  504.9 3.7 reshape.112
  508.6 1.9 convolution_convert_fusion
  510.5 1.7 fusion.43
  512.7 2.1 collective-permute-start.1
  516.1 2.1 collective-permute-start.3
  518.2 2.1 collective-permute-start.4
  520.3 2.1 collective-permute-start.5
  522.4 2.1 collective-permute-start.6
  525.3 2.1 collective-permute-start.7
  528.6 6.0 collective-permute-done.4
  534.6 6.0 collective-permute-done.5
  540.6 1.7 fusion.36
  543.3 15.7 %all_to_all.10 = bf16[32,2,2048]{2,1,0:T(2,128)(2,1)} all-to-all(bf16[32,2,2048]{2,1,0:T(2,128)(2,1)S(1)} %reshape.117), channel_id=1, replica_groups=mesh['section'=8,'expert'=32] {'expert'}, dimensions={0} | all-to-all | bytes 524288 | tf_op jit(solution)/shard_map/all_to_all | solution.py:93
  559.2 24.6 %all-gather.8.cloned.1.call-done = bf16[256,2,2048]{2,1,0:T(2,128)(2,1)} async-done(((bf16[32,2,2048]{2,1,0:T(2,128)(2,1)}), bf16[256,2,2048]{2,1,0:T(2,128)(2,1)}) %all-gather.8.cloned.1.call-update) | async-done | bytes 2097168 | tf_op jit(solution)/shard_map/all_gather | solution.py:94
  583.8 2.7 reshape.118
  588.0 4.9 multiply_convert_fusion.2
  593.0 36.3 %reduce-scatter.2.cloned.1.call-done = bf16[512,256]{1,0:T(8,128)(2,1)} async-done(((bf16[512,2048]{1,0:T(8,128)(2,1)}), bf16[512,256]{1,0:T(8,128)(2,1)}) %reduce-scatter.2.cloned.1.call-update) | async-done | bytes 262160 | tf_op jit(solution)/shard_map/reduce_scatter | solution.py:105
  631.2 9.3 %all-to-all-start.1 = ((bf16[32,8,2,256]{3,2,1,0:T(2,128)(2,1)}), bf16[32,8,2,256]{3,2,1,0:T(2,128)(2,1)S(1)}, u32[]{:S(2)}, u32[]{:S(2)}) async-start(bf16[32,8,2,256]{3,2,1,0:T(2,128)(2,1)} %bitcast.85), calls=%async_computation.2 | async-start | bytes 524288 | tf_op jit(solution)/shard_map/all_to_all | solution.py:107
  640.7 12.6 %all-to-all-done.1 = bf16[32,8,2,256]{3,2,1,0:T(2,128)(2,1)S(1)} async-done(((bf16[32,8,2,256]{3,2,1,0:T(2,128)(2,1)}), bf16[32,8,2,256]{3,2,1,0:T(2,128)(2,1)S(1)}, u32[]{:S(2)}, u32[]{:S(2)}) %all-to-all-start.1) | async-done | bytes 262176 | tf_op jit(solution)/shard_map/all_to_all | solution.py:107
  653.4 2.1 scatter_custom_fusion
  (124 shorter events, 77.6 us)
Async XLA Ops:
  6.5 581.4 %copy-start = (bf16[1,256,2048]{2,1,0:T(8,128)(2,1)S(1)}, bf16[1,256,2048]{2,1,0:T(8,128)(2,1)}, u32[]{:S(2)}) copy-start(bf16[1,256,2048]{2,1,0:T(8,128)(2,1)} %param.17) | copy-start | bytes 3145732
  6.5 103.5 %all-gather.4.cloned.1.call-start = ((), (), s32[]{:S(2)}) async-start(), calls=%async_computation.3 | async-start | bytes 8650752 | tf_op jit(solution)/shard_map/all_gather | solution.py:35
  7.3 200.3 %all-gather.6.cloned.1.call-start = ((), (), s32[]{:S(2)}) async-start(), calls=%async_computation.4 | async-start | bytes 8650752 | tf_op jit(solution)/shard_map/all_gather | solution.py:36
  8.0 575.8 %all-gather.8.cloned.1.call-start = ((), (), s32[]{:S(2)}) async-start(), calls=%async_computation.5 | async-start | bytes 2359296 | tf_op jit(solution)/shard_map/all_gather | solution.py:94
  210.1 4.7 collective-permute-start
  216.3 8.3 %collective-permute-start = (bf16[72,2048]{1,0:T(8,128)(2,1)}, bf16[72,2048]{1,0:T(8,128)(2,1)}, u32[]{:S(2)}, u32[]{:S(2)}) collective-permute-start(bf16[72,2048]{1,0:T(8,128)(2,1)} %get-tuple-element.294), channel_id=1, source_target_pairs={{0,32},{32,64},{64,96},{96,128},{128,160},{160,192},{192,224},{1,3... | collective-permute-start | bytes 884744 | tf_op jit(solution)/shard_map/while/body/eval_jaxpr/ppermute | solution.py:10
  226.1 8.3 %collective-permute-start = (bf16[72,2048]{1,0:T(8,128)(2,1)}, bf16[72,2048]{1,0:T(8,128)(2,1)}, u32[]{:S(2)}, u32[]{:S(2)}) collective-permute-start(bf16[72,2048]{1,0:T(8,128)(2,1)} %get-tuple-element.294), channel_id=1, source_target_pairs={{0,32},{32,64},{64,96},{96,128},{128,160},{160,192},{192,224},{1,3... | collective-permute-start | bytes 884744 | tf_op jit(solution)/shard_map/while/body/eval_jaxpr/ppermute | solution.py:10
  236.0 8.3 %collective-permute-start = (bf16[72,2048]{1,0:T(8,128)(2,1)}, bf16[72,2048]{1,0:T(8,128)(2,1)}, u32[]{:S(2)}, u32[]{:S(2)}) collective-permute-start(bf16[72,2048]{1,0:T(8,128)(2,1)} %get-tuple-element.294), channel_id=1, source_target_pairs={{0,32},{32,64},{64,96},{96,128},{128,160},{160,192},{192,224},{1,3... | collective-permute-start | bytes 884744 | tf_op jit(solution)/shard_map/while/body/eval_jaxpr/ppermute | solution.py:10
  245.8 8.3 %collective-permute-start = (bf16[72,2048]{1,0:T(8,128)(2,1)}, bf16[72,2048]{1,0:T(8,128)(2,1)}, u32[]{:S(2)}, u32[]{:S(2)}) collective-permute-start(bf16[72,2048]{1,0:T(8,128)(2,1)} %get-tuple-element.294), channel_id=1, source_target_pairs={{0,32},{32,64},{64,96},{96,128},{128,160},{160,192},{192,224},{1,3... | collective-permute-start | bytes 884744 | tf_op jit(solution)/shard_map/while/body/eval_jaxpr/ppermute | solution.py:10
  255.6 8.3 %collective-permute-start = (bf16[72,2048]{1,0:T(8,128)(2,1)}, bf16[72,2048]{1,0:T(8,128)(2,1)}, u32[]{:S(2)}, u32[]{:S(2)}) collective-permute-start(bf16[72,2048]{1,0:T(8,128)(2,1)} %get-tuple-element.294), channel_id=1, source_target_pairs={{0,32},{32,64},{64,96},{96,128},{128,160},{160,192},{192,224},{1,3... | collective-permute-start | bytes 884744 | tf_op jit(solution)/shard_map/while/body/eval_jaxpr/ppermute | solution.py:10
  265.4 68.8 %collective-permute-start = (bf16[72,2048]{1,0:T(8,128)(2,1)}, bf16[72,2048]{1,0:T(8,128)(2,1)}, u32[]{:S(2)}, u32[]{:S(2)}) collective-permute-start(bf16[72,2048]{1,0:T(8,128)(2,1)} %get-tuple-element.294), channel_id=1, source_target_pairs={{0,32},{32,64},{64,96},{96,128},{128,160},{160,192},{192,224},{1,3... | collective-permute-start | bytes 884744 | tf_op jit(solution)/shard_map/while/body/eval_jaxpr/ppermute | solution.py:10
  347.1 8.4 %collective-permute-start = (bf16[72,2048]{1,0:T(8,128)(2,1)}, bf16[72,2048]{1,0:T(8,128)(2,1)}, u32[]{:S(2)}, u32[]{:S(2)}) collective-permute-start(bf16[72,2048]{1,0:T(8,128)(2,1)} %get-tuple-element.294), channel_id=1, source_target_pairs={{0,32},{32,64},{64,96},{96,128},{128,160},{160,192},{192,224},{1,3... | collective-permute-start | bytes 884744 | tf_op jit(solution)/shard_map/while/body/eval_jaxpr/ppermute | solution.py:10
  368.3 8.3 %collective-permute-start = (bf16[72,2048]{1,0:T(8,128)(2,1)}, bf16[72,2048]{1,0:T(8,128)(2,1)}, u32[]{:S(2)}, u32[]{:S(2)}) collective-permute-start(bf16[72,2048]{1,0:T(8,128)(2,1)} %get-tuple-element.294), channel_id=1, source_target_pairs={{0,32},{32,64},{64,96},{96,128},{128,160},{160,192},{192,224},{1,3... | collective-permute-start | bytes 884744 | tf_op jit(solution)/shard_map/while/body/eval_jaxpr/ppermute | solution.py:10
  389.4 8.3 %collective-permute-start = (bf16[72,2048]{1,0:T(8,128)(2,1)}, bf16[72,2048]{1,0:T(8,128)(2,1)}, u32[]{:S(2)}, u32[]{:S(2)}) collective-permute-start(bf16[72,2048]{1,0:T(8,128)(2,1)} %get-tuple-element.294), channel_id=1, source_target_pairs={{0,32},{32,64},{64,96},{96,128},{128,160},{160,192},{192,224},{1,3... | collective-permute-start | bytes 884744 | tf_op jit(solution)/shard_map/while/body/eval_jaxpr/ppermute | solution.py:10
  410.6 8.3 %collective-permute-start = (bf16[72,2048]{1,0:T(8,128)(2,1)}, bf16[72,2048]{1,0:T(8,128)(2,1)}, u32[]{:S(2)}, u32[]{:S(2)}) collective-permute-start(bf16[72,2048]{1,0:T(8,128)(2,1)} %get-tuple-element.294), channel_id=1, source_target_pairs={{0,32},{32,64},{64,96},{96,128},{128,160},{160,192},{192,224},{1,3... | collective-permute-start | bytes 884744 | tf_op jit(solution)/shard_map/while/body/eval_jaxpr/ppermute | solution.py:10
  431.7 8.3 %collective-permute-start = (bf16[72,2048]{1,0:T(8,128)(2,1)}, bf16[72,2048]{1,0:T(8,128)(2,1)}, u32[]{:S(2)}, u32[]{:S(2)}) collective-permute-start(bf16[72,2048]{1,0:T(8,128)(2,1)} %get-tuple-element.294), channel_id=1, source_target_pairs={{0,32},{32,64},{64,96},{96,128},{128,160},{160,192},{192,224},{1,3... | collective-permute-start | bytes 884744 | tf_op jit(solution)/shard_map/while/body/eval_jaxpr/ppermute | solution.py:10
  452.9 8.3 %collective-permute-start = (bf16[72,2048]{1,0:T(8,128)(2,1)}, bf16[72,2048]{1,0:T(8,128)(2,1)}, u32[]{:S(2)}, u32[]{:S(2)}) collective-permute-start(bf16[72,2048]{1,0:T(8,128)(2,1)} %get-tuple-element.294), channel_id=1, source_target_pairs={{0,32},{32,64},{64,96},{96,128},{128,160},{160,192},{192,224},{1,3... | collective-permute-start | bytes 884744 | tf_op jit(solution)/shard_map/while/body/eval_jaxpr/ppermute | solution.py:10
  474.0 8.3 %collective-permute-start = (bf16[72,2048]{1,0:T(8,128)(2,1)}, bf16[72,2048]{1,0:T(8,128)(2,1)}, u32[]{:S(2)}, u32[]{:S(2)}) collective-permute-start(bf16[72,2048]{1,0:T(8,128)(2,1)} %get-tuple-element.294), channel_id=1, source_target_pairs={{0,32},{32,64},{64,96},{96,128},{128,160},{160,192},{192,224},{1,3... | collective-permute-start | bytes 884744 | tf_op jit(solution)/shard_map/while/body/eval_jaxpr/ppermute | solution.py:10
  495.2 3.8 collective-permute-start
  510.4 2.3 copy-start.1
  512.7 9.7 %collective-permute-start.1 = (bf16[136,2048]{1,0:T(8,128)(2,1)S(1)}, bf16[136,2048]{1,0:T(8,128)(2,1)S(1)}, u32[]{:S(2)}, u32[]{:S(2)}) collective-permute-start(bf16[136,2048]{1,0:T(8,128)(2,1)S(1)} %get-tuple-element.231), channel_id=1, source_target_pairs={{224,192},{225,193},{226,194},{227,195},{228,196},{229,197},{230,1... | collective-permute-start | bytes 1671176 | tf_op jit(solution)/shard_map/ppermute | solution.py:88
  514.8 9.7 %collective-permute-start.2 = (bf16[136,2048]{1,0:T(8,128)(2,1)S(1)}, bf16[136,2048]{1,0:T(8,128)(2,1)S(1)}, u32[]{:S(2)}, u32[]{:S(2)}) collective-permute-start(bf16[136,2048]{1,0:T(8,128)(2,1)S(1)} %get-tuple-element.232), channel_id=1, source_target_pairs={{224,160},{225,161},{226,162},{227,163},{228,164},{229,165},{230,1... | collective-permute-start | bytes 1671176 | tf_op jit(solution)/shard_map/ppermute | solution.py:88
  516.1 12.5 %collective-permute-start.3 = (bf16[136,2048]{1,0:T(8,128)(2,1)}, bf16[136,2048]{1,0:T(8,128)(2,1)}, u32[]{:S(2)}, u32[]{:S(2)}) collective-permute-start(bf16[136,2048]{1,0:T(8,128)(2,1)} %get-tuple-element.233), channel_id=1, source_target_pairs={{224,128},{225,129},{226,130},{227,131},{228,132},{229,133},{230,1... | collective-permute-start | bytes 1671176 | tf_op jit(solution)/shard_map/ppermute | solution.py:88
  518.2 16.3 %collective-permute-start.4 = (bf16[136,2048]{1,0:T(8,128)(2,1)}, bf16[136,2048]{1,0:T(8,128)(2,1)}, u32[]{:S(2)}, u32[]{:S(2)}) collective-permute-start(bf16[136,2048]{1,0:T(8,128)(2,1)} %get-tuple-element.234), channel_id=1, source_target_pairs={{224,96},{225,97},{226,98},{227,99},{228,100},{229,101},{230,102},... | collective-permute-start | bytes 1671176 | tf_op jit(solution)/shard_map/ppermute | solution.py:88
  520.3 20.2 %collective-permute-start.5 = (bf16[136,2048]{1,0:T(8,128)(2,1)}, bf16[136,2048]{1,0:T(8,128)(2,1)}, u32[]{:S(2)}, u32[]{:S(2)}) collective-permute-start(bf16[136,2048]{1,0:T(8,128)(2,1)} %get-tuple-element.235), channel_id=1, source_target_pairs={{224,64},{225,65},{226,66},{227,67},{228,68},{229,69},{230,70},{23... | collective-permute-start | bytes 1671176 | tf_op jit(solution)/shard_map/ppermute | solution.py:88
  522.4 2.1 copy-start.4
  522.4 18.1 %collective-permute-start.6 = (bf16[136,2048]{1,0:T(8,128)(2,1)}, bf16[136,2048]{1,0:T(8,128)(2,1)}, u32[]{:S(2)}, u32[]{:S(2)}) collective-permute-start(bf16[136,2048]{1,0:T(8,128)(2,1)} %get-tuple-element.236), channel_id=1, source_target_pairs={{224,32},{225,33},{226,34},{227,35},{228,36},{229,37},{230,38},{23... | collective-permute-start | bytes 1671176 | tf_op jit(solution)/shard_map/ppermute | solution.py:88
  524.5 0.8 copy-start.5
  525.3 15.2 %collective-permute-start.7 = (bf16[136,2048]{1,0:T(8,128)(2,1)}, bf16[136,2048]{1,0:T(8,128)(2,1)}, u32[]{:S(2)}, u32[]{:S(2)}) collective-permute-start(bf16[136,2048]{1,0:T(8,128)(2,1)} %get-tuple-element.230), channel_id=1, source_target_pairs={{224,0},{225,1},{226,2},{227,3},{228,4},{229,5},{230,6},{231,7},{2... | collective-permute-start | bytes 1671176 | tf_op jit(solution)/shard_map/ppermute | solution.py:88
  542.3 0.8 copy-start.2
  559.0 70.3 %reduce-scatter.2.cloned.1.call-start = ((), (), s32[]{:S(2)}) async-start(), calls=%async_computation.6 | async-start | bytes 2359296 | tf_op jit(solution)/shard_map/reduce_scatter | solution.py:105
  588.0 4.9 copy-start.6
  592.9 47.7 %copy-start.3 = (bf16[136,2048]{1,0:T(8,128)(2,1)S(1)}, bf16[136,2048]{1,0:T(8,128)(2,1)}, u32[]{:S(2)}) copy-start(bf16[136,2048]{1,0:T(8,128)(2,1)} %copy-done.2) | copy-start | bytes 1671172
  631.2 22.1 %all-to-all-start.1 = ((bf16[32,8,2,256]{3,2,1,0:T(2,128)(2,1)}), bf16[32,8,2,256]{3,2,1,0:T(2,128)(2,1)S(1)}, u32[]{:S(2)}, u32[]{:S(2)}) async-start(bf16[32,8,2,256]{3,2,1,0:T(2,128)(2,1)} %bitcast.85), calls=%async_computation.2 | async-start | bytes 524288 | tf_op jit(solution)/shard_map/all_to_all | solution.py:107
Sparse Core Ops, SparseCore 0:
  9.9 100.0 all-gather.3
  112.6 94.9 all-gather.5
  559.1 24.6 all-gather.7
  593.0 36.1 reduce-scatter.1
where the time goes:
time: 665 us; the launch traced here: 663 us
  waiting for transfers between devices  432 us (65%)
  matrix products  87 us (13%)
  starting transfers between devices  42.7 us (6%)
  local copies, waits for them, and re-layouts  40.5 us (6%)
  other arithmetic  31.2 us (5%)
  blocking collectives  15.7 us (2%)
  between operations  13.3 us (2%)
    ppermute x15, waiting for transfers between devices, from_behind(): lax.ppermute(value, axis, [(source, source + steps) for source in range(i...  149 us
    all_gather x1, waiting for transfers between devices, local(): lax.all_gather(w_out, 'expert', axis=1, tiled=True)  97.6 us
    all_gather x1, waiting for transfers between devices, local(): lax.all_gather(w_in, 'expert', axis=1, tiled=True)  97.6 us
    dot_general x8, matrix products, processor(): branch = jnp.dot(hidden, w_second, preferred_element_type=jnp.float32)  78.8 us
    reduce_scatter x1, waiting for transfers between devices, local(): lax.psum_scatter(scaled, 'section', scatter_dimension=1, tiled=True)  36.3 us
    all_gather x1, waiting for transfers between devices, local(): lax.all_gather(arrived, 'section', axis=0, tiled=True).reshape(-1, width)  24.6 us
    ppermute x15, starting transfers between devices, from_behind(): lax.ppermute(value, axis, [(source, source + steps) for source in range(i...  19.2 us
    all_to_all x1, blocking collectives, local(): lax.all_to_all(outgoing, 'expert', split_axis=0, concat_axis=0, tiled=True)  15.7 us
  transfers between devices with their start and end apart: 27, of which 23 were waited for; matrix products, arithmetic and copies ran while one was open for 2% of the time, Pallas kernels for 0%

commit v1 on v0

--- a/solution.py
+++ b/solution.py
@@ -33,7 +33,9 @@
     micro, tok_dev, width = tokens.shape
     w_first, w_second = (
         lax.all_gather(w_in, "expert", axis=1, tiled=True),
-        lax.all_gather(w_out, "expert", axis=1, tiled=True),
+        jnp.concatenate(
+            lax.all_to_all(jnp.stack([w_out] * lax.axis_size("expert")), "expert", 0, 0), axis=1
+        ),
     )
     w_first = w_first[0]
     w_second = w_second[0]

time: 665 us -> 717 us (1.078)
  waiting for transfers between devices: 432 us -> 466 us
  starting transfers between devices: 42.7 us -> 54.2 us
    all_to_all x0 -> x1, waiting for transfers between devices: none -> 229 us  [local(): lax.all_to_all(jnp.stack([w_out] * lax.axis_size('expert')), 'expert', 0, 0)]
    all_gather x1 -> x0, waiting for transfers between devices: 97.6 us -> none  [local(): lax.all_gather(w_out, 'expert', axis=1, tiled=True)]
    all_gather x1, waiting for transfers between devices: 97.6 us -> 0.01 us  [local(): lax.all_gather(w_in, 'expert', axis=1, tiled=True)]
    all_to_all x0 -> x1, starting transfers between devices: none -> 11.5 us  [local(): lax.all_to_all(jnp.stack([w_out] * lax.axis_size('expert')), 'expert', 0, 0)]
  transfers between devices with their start and end apart: 27 -> 27, of which waited for: 23 -> 22; matrix products, arithmetic and copies ran while one was open for 2% -> 1% of each run, Pallas kernels for 0% -> 0%
where the time goes in v1:
time: 717 us; the launch traced here: 715 us
  waiting for transfers between devices  466 us (65%)
  matrix products  87 us (12%)
  starting transfers between devices  54.2 us (8%)
  local copies, waits for them, and re-layouts  45.8 us (6%)
  other arithmetic  27.7 us (4%)
  blocking collectives  20.7 us (3%)
  between operations  13.4 us (2%)
    all_to_all x1, waiting for transfers between devices, local(): lax.all_to_all(jnp.stack([w_out] * lax.axis_size('expert')), 'expert', 0, 0)  229 us
    ppermute x15, waiting for transfers between devices, from_behind(): lax.ppermute(value, axis, [(source, source + steps) for source in range(i...  149 us
    dot_general x8, matrix products, processor(): branch = jnp.dot(hidden, w_second, preferred_element_type=jnp.float32)  78.8 us
    reduce_scatter x1, waiting for transfers between devices, local(): lax.psum_scatter(scaled, 'section', scatter_dimension=1, tiled=True)  36.3 us
    all_gather x1, waiting for transfers between devices, local(): lax.all_gather(arrived, 'section', axis=0, tiled=True).reshape(-1, width)  24.6 us
    all_to_all x1, blocking collectives, local(): lax.all_to_all(outgoing, 'expert', split_axis=0, concat_axis=0, tiled=True)  20.7 us
    ppermute x15, starting transfers between devices, from_behind(): lax.ppermute(value, axis, [(source, source + steps) for source in range(i...  19.2 us
  transfers between devices with their start and end apart: 27, of which 22 were waited for; matrix products, arithmetic and copies ran while one was open for 1% of the time, Pallas kernels for 0%

profile of v1, /device:TPU:7, one launch (start us, length us, event | category | flops | bytes accessed | tf_op | source)
XLA Modules:
  0.0 715.0 jit_solution(4653836272457592735)
XLA Ops:
  6.5 5.3 stack.2
  11.9 11.5 %all-to-all-start = ((bf16[32,1,64,2048]{3,2,1,0:T(8,128)(2,1)}), bf16[32,1,64,2048]{3,2,1,0:T(8,128)(2,1)}, u32[]{:S(2)}, u32[]{:S(2)}) async-start(bf16[32,1,64,2048]{3,2,1,0:T(8,128)(2,1)} %stack.2), calls=%async_computation | async-start | bytes 16777216 | tf_op jit(solution)/shard_map/all_to_all | solution.py:37
  25.2 229.0 %all-to-all-done = bf16[32,1,64,2048]{3,2,1,0:T(8,128)(2,1)} async-done(((bf16[32,1,64,2048]{3,2,1,0:T(8,128)(2,1)}), bf16[32,1,64,2048]{3,2,1,0:T(8,128)(2,1)}, u32[]{:S(2)}, u32[]{:S(2)}) %all-to-all-start) | async-done | bytes 8388640 | tf_op jit(solution)/shard_map/all_to_all | solution.py:37
  255.2 291.0 %while.16 = (s32[]{:T(128)}, bf16[72,2048]{1,0:T(8,128)(2,1)}, bf16[8,72,2048]{2,1,0:T(8,128)(2,1)S(1)}, s32[]{:T(128)}, pred[]{:T(512)}, /*index=5*/bf16[8,72,2...) while((s32[]{:T(128)}, bf16[72,2048]{1,0:T(8,128)(2,1)}, ...), condition=%wide.region_4.5_spmd, body=%wide.region_0.4_spmd.sunk | while | flops 1210613888 | bytes 21499308 | solution.py:64
  258.1 4.0 collective-permute-done
  265.0 6.9 collective-permute-done
  274.8 6.9 collective-permute-done
  284.6 6.9 collective-permute-done
  294.5 6.9 collective-permute-done
  304.3 6.9 collective-permute-done
  314.1 67.4 %collective-permute-done = bf16[72,2048]{1,0:T(8,128)(2,1)} collective-permute-done((bf16[72,2048]{1,0:T(8,128)(2,1)}, bf16[72,2048]{1,0:T(8,128)(2,1)}, u32[]{:S(2)}, u32[]{:S(2)}) %collective-permute-start) | collective-permute-done | bytes 294944 | tf_op jit(solution)/shard_map/while/body/eval_jaxpr/ppermute | solution.py:10
  381.5 12.8 %conditional.2 = (bf16[72,2048]{1,0:T(8,128)(2,1)}, bf16[1,72,2048]{2,1,0:T(8,128)(2,1)}) conditional(s32[]{:T(128)} %convert_element_type.108, () %tuple.53, (pred[]{:T(512)}, bf16[8,72,2048]{2,1,0:T(8,128)(2,1)}, s32[]{:T(128)}, bf16[72,2048]{1,0:T(8,128)(2,1)}, bf16[2048,2048]{1,0:T(8,128)(2,1)}, /*index=5*/bf16[2048,2048]{1,0:T(8,128)(2,1)}) %tuple.54), branch_computations={%region_1.1_spmd, %region_2.3_spmd} | conditional | flops 1210466432 | bytes 19434644 | solution.py:57
  382.8 9.8 %fusion = bf16[72,2048]{1,0:T(8,128)(2,1)} fusion(bf16[2048,2048]{1,0:T(8,128)(2,1)} %get-tuple-element.195, bf16[2048,2048]{1,0:T(8,128)(2,1)} %get-tuple-element.194, f32[72]{0:T(128)S(1)} %add_rsqrt_fusion, bf16[72,2048]{1,0:T(8,128)(2,1)} %get-tuple-element.193, bf16[8,72,2048]{2,1,0:T(8,128)(2,1)} %get-tuple-element.191, s32[]{:T(128)} %get-tuple-element.192, ...), kind=kOutput, calls=%fused_computation.4 | convolution fusion | flops 1209876480 | bytes 18254112 | tf_op jit(solution)/shard_map/while/body/eval_jaxpr/cond/branch_1_fun/dot_general | solution.py:24
  392.6 1.7 copy.30
  396.7 6.0 collective-permute-done
  402.7 12.8 %conditional.2 = (bf16[72,2048]{1,0:T(8,128)(2,1)}, bf16[1,72,2048]{2,1,0:T(8,128)(2,1)}) conditional(s32[]{:T(128)} %convert_element_type.108, () %tuple.53, (pred[]{:T(512)}, bf16[8,72,2048]{2,1,0:T(8,128)(2,1)}, s32[]{:T(128)}, bf16[72,2048]{1,0:T(8,128)(2,1)}, bf16[2048,2048]{1,0:T(8,128)(2,1)}, /*index=5*/bf16[2048,2048]{1,0:T(8,128)(2,1)}) %tuple.54), branch_computations={%region_1.1_spmd, %region_2.3_spmd} | conditional | flops 1210466432 | bytes 19434644 | solution.py:57
  403.9 9.8 %fusion = bf16[72,2048]{1,0:T(8,128)(2,1)} fusion(bf16[2048,2048]{1,0:T(8,128)(2,1)} %get-tuple-element.195, bf16[2048,2048]{1,0:T(8,128)(2,1)} %get-tuple-element.194, f32[72]{0:T(128)S(1)} %add_rsqrt_fusion, bf16[72,2048]{1,0:T(8,128)(2,1)} %get-tuple-element.193, bf16[8,72,2048]{2,1,0:T(8,128)(2,1)} %get-tuple-element.191, s32[]{:T(128)} %get-tuple-element.192, ...), kind=kOutput, calls=%fused_computation.4 | convolution fusion | flops 1209876480 | bytes 18254112 | tf_op jit(solution)/shard_map/while/body/eval_jaxpr/cond/branch_1_fun/dot_general | solution.py:24
  413.8 1.7 copy.30
  417.8 6.0 collective-permute-done
  423.8 12.8 %conditional.2 = (bf16[72,2048]{1,0:T(8,128)(2,1)}, bf16[1,72,2048]{2,1,0:T(8,128)(2,1)}) conditional(s32[]{:T(128)} %convert_element_type.108, () %tuple.53, (pred[]{:T(512)}, bf16[8,72,2048]{2,1,0:T(8,128)(2,1)}, s32[]{:T(128)}, bf16[72,2048]{1,0:T(8,128)(2,1)}, bf16[2048,2048]{1,0:T(8,128)(2,1)}, /*index=5*/bf16[2048,2048]{1,0:T(8,128)(2,1)}) %tuple.54), branch_computations={%region_1.1_spmd, %region_2.3_spmd} | conditional | flops 1210466432 | bytes 19434644 | solution.py:57
  425.1 9.8 %fusion = bf16[72,2048]{1,0:T(8,128)(2,1)} fusion(bf16[2048,2048]{1,0:T(8,128)(2,1)} %get-tuple-element.195, bf16[2048,2048]{1,0:T(8,128)(2,1)} %get-tuple-element.194, f32[72]{0:T(128)S(1)} %add_rsqrt_fusion, bf16[72,2048]{1,0:T(8,128)(2,1)} %get-tuple-element.193, bf16[8,72,2048]{2,1,0:T(8,128)(2,1)} %get-tuple-element.191, s32[]{:T(128)} %get-tuple-element.192, ...), kind=kOutput, calls=%fused_computation.4 | convolution fusion | flops 1209876480 | bytes 18254112 | tf_op jit(solution)/shard_map/while/body/eval_jaxpr/cond/branch_1_fun/dot_general | solution.py:24
  434.9 1.7 copy.30
  439.0 6.0 collective-permute-done
  445.0 12.8 %conditional.2 = (bf16[72,2048]{1,0:T(8,128)(2,1)}, bf16[1,72,2048]{2,1,0:T(8,128)(2,1)}) conditional(s32[]{:T(128)} %convert_element_type.108, () %tuple.53, (pred[]{:T(512)}, bf16[8,72,2048]{2,1,0:T(8,128)(2,1)}, s32[]{:T(128)}, bf16[72,2048]{1,0:T(8,128)(2,1)}, bf16[2048,2048]{1,0:T(8,128)(2,1)}, /*index=5*/bf16[2048,2048]{1,0:T(8,128)(2,1)}) %tuple.54), branch_computations={%region_1.1_spmd, %region_2.3_spmd} | conditional | flops 1210466432 | bytes 19434644 | solution.py:57
  446.2 9.8 %fusion = bf16[72,2048]{1,0:T(8,128)(2,1)} fusion(bf16[2048,2048]{1,0:T(8,128)(2,1)} %get-tuple-element.195, bf16[2048,2048]{1,0:T(8,128)(2,1)} %get-tuple-element.194, f32[72]{0:T(128)S(1)} %add_rsqrt_fusion, bf16[72,2048]{1,0:T(8,128)(2,1)} %get-tuple-element.193, bf16[8,72,2048]{2,1,0:T(8,128)(2,1)} %get-tuple-element.191, s32[]{:T(128)} %get-tuple-element.192, ...), kind=kOutput, calls=%fused_computation.4 | convolution fusion | flops 1209876480 | bytes 18254112 | tf_op jit(solution)/shard_map/while/body/eval_jaxpr/cond/branch_1_fun/dot_general | solution.py:24
  456.1 1.7 copy.30
  460.1 6.0 collective-permute-done
  466.1 12.8 %conditional.2 = (bf16[72,2048]{1,0:T(8,128)(2,1)}, bf16[1,72,2048]{2,1,0:T(8,128)(2,1)}) conditional(s32[]{:T(128)} %convert_element_type.108, () %tuple.53, (pred[]{:T(512)}, bf16[8,72,2048]{2,1,0:T(8,128)(2,1)}, s32[]{:T(128)}, bf16[72,2048]{1,0:T(8,128)(2,1)}, bf16[2048,2048]{1,0:T(8,128)(2,1)}, /*index=5*/bf16[2048,2048]{1,0:T(8,128)(2,1)}) %tuple.54), branch_computations={%region_1.1_spmd, %region_2.3_spmd} | conditional | flops 1210466432 | bytes 19434644 | solution.py:57
  467.4 9.8 %fusion = bf16[72,2048]{1,0:T(8,128)(2,1)} fusion(bf16[2048,2048]{1,0:T(8,128)(2,1)} %get-tuple-element.195, bf16[2048,2048]{1,0:T(8,128)(2,1)} %get-tuple-element.194, f32[72]{0:T(128)S(1)} %add_rsqrt_fusion, bf16[72,2048]{1,0:T(8,128)(2,1)} %get-tuple-element.193, bf16[8,72,2048]{2,1,0:T(8,128)(2,1)} %get-tuple-element.191, s32[]{:T(128)} %get-tuple-element.192, ...), kind=kOutput, calls=%fused_computation.4 | convolution fusion | flops 1209876480 | bytes 18254112 | tf_op jit(solution)/shard_map/while/body/eval_jaxpr/cond/branch_1_fun/dot_general | solution.py:24
  477.2 1.7 copy.30
  481.3 6.0 collective-permute-done
  487.3 12.8 %conditional.2 = (bf16[72,2048]{1,0:T(8,128)(2,1)}, bf16[1,72,2048]{2,1,0:T(8,128)(2,1)}) conditional(s32[]{:T(128)} %convert_element_type.108, () %tuple.53, (pred[]{:T(512)}, bf16[8,72,2048]{2,1,0:T(8,128)(2,1)}, s32[]{:T(128)}, bf16[72,2048]{1,0:T(8,128)(2,1)}, bf16[2048,2048]{1,0:T(8,128)(2,1)}, /*index=5*/bf16[2048,2048]{1,0:T(8,128)(2,1)}) %tuple.54), branch_computations={%region_1.1_spmd, %region_2.3_spmd} | conditional | flops 1210466432 | bytes 19434644 | solution.py:57
  488.6 9.8 %fusion = bf16[72,2048]{1,0:T(8,128)(2,1)} fusion(bf16[2048,2048]{1,0:T(8,128)(2,1)} %get-tuple-element.195, bf16[2048,2048]{1,0:T(8,128)(2,1)} %get-tuple-element.194, f32[72]{0:T(128)S(1)} %add_rsqrt_fusion, bf16[72,2048]{1,0:T(8,128)(2,1)} %get-tuple-element.193, bf16[8,72,2048]{2,1,0:T(8,128)(2,1)} %get-tuple-element.191, s32[]{:T(128)} %get-tuple-element.192, ...), kind=kOutput, calls=%fused_computation.4 | convolution fusion | flops 1209876480 | bytes 18254112 | tf_op jit(solution)/shard_map/while/body/eval_jaxpr/cond/branch_1_fun/dot_general | solution.py:24
  498.4 1.7 copy.30
  502.5 6.0 collective-permute-done
  508.4 12.8 %conditional.2 = (bf16[72,2048]{1,0:T(8,128)(2,1)}, bf16[1,72,2048]{2,1,0:T(8,128)(2,1)}) conditional(s32[]{:T(128)} %convert_element_type.108, () %tuple.53, (pred[]{:T(512)}, bf16[8,72,2048]{2,1,0:T(8,128)(2,1)}, s32[]{:T(128)}, bf16[72,2048]{1,0:T(8,128)(2,1)}, bf16[2048,2048]{1,0:T(8,128)(2,1)}, /*index=5*/bf16[2048,2048]{1,0:T(8,128)(2,1)}) %tuple.54), branch_computations={%region_1.1_spmd, %region_2.3_spmd} | conditional | flops 1210466432 | bytes 19434644 | solution.py:57
  509.7 9.8 %fusion = bf16[72,2048]{1,0:T(8,128)(2,1)} fusion(bf16[2048,2048]{1,0:T(8,128)(2,1)} %get-tuple-element.195, bf16[2048,2048]{1,0:T(8,128)(2,1)} %get-tuple-element.194, f32[72]{0:T(128)S(1)} %add_rsqrt_fusion, bf16[72,2048]{1,0:T(8,128)(2,1)} %get-tuple-element.193, bf16[8,72,2048]{2,1,0:T(8,128)(2,1)} %get-tuple-element.191, s32[]{:T(128)} %get-tuple-element.192, ...), kind=kOutput, calls=%fused_computation.4 | convolution fusion | flops 1209876480 | bytes 18254112 | tf_op jit(solution)/shard_map/while/body/eval_jaxpr/cond/branch_1_fun/dot_general | solution.py:24
  519.6 1.7 copy.30
  523.6 6.0 collective-permute-done
  529.6 12.8 %conditional.2 = (bf16[72,2048]{1,0:T(8,128)(2,1)}, bf16[1,72,2048]{2,1,0:T(8,128)(2,1)}) conditional(s32[]{:T(128)} %convert_element_type.108, () %tuple.53, (pred[]{:T(512)}, bf16[8,72,2048]{2,1,0:T(8,128)(2,1)}, s32[]{:T(128)}, bf16[72,2048]{1,0:T(8,128)(2,1)}, bf16[2048,2048]{1,0:T(8,128)(2,1)}, /*index=5*/bf16[2048,2048]{1,0:T(8,128)(2,1)}) %tuple.54), branch_computations={%region_1.1_spmd, %region_2.3_spmd} | conditional | flops 1210466432 | bytes 19434644 | solution.py:57
  530.9 9.8 %fusion = bf16[72,2048]{1,0:T(8,128)(2,1)} fusion(bf16[2048,2048]{1,0:T(8,128)(2,1)} %get-tuple-element.195, bf16[2048,2048]{1,0:T(8,128)(2,1)} %get-tuple-element.194, f32[72]{0:T(128)S(1)} %add_rsqrt_fusion, bf16[72,2048]{1,0:T(8,128)(2,1)} %get-tuple-element.193, bf16[8,72,2048]{2,1,0:T(8,128)(2,1)} %get-tuple-element.191, s32[]{:T(128)} %get-tuple-element.192, ...), kind=kOutput, calls=%fused_computation.4 | convolution fusion | flops 1209876480 | bytes 18254112 | tf_op jit(solution)/shard_map/while/body/eval_jaxpr/cond/branch_1_fun/dot_general | solution.py:24
  540.7 1.7 copy.30
  546.2 1.8 gather_fusion
  550.2 1.9 copy.25
  552.1 3.7 reshape.115
  555.8 1.9 convolution_convert_fusion
  557.7 1.7 fusion.43
  559.9 2.1 collective-permute-start.1
  563.3 2.1 collective-permute-start.3
  565.4 2.1 collective-permute-start.4
  567.5 2.1 collective-permute-start.5
  569.6 2.1 collective-permute-start.6
  572.6 2.1 collective-permute-start.7
  575.8 6.0 collective-permute-done.4
  581.8 6.0 collective-permute-done.5
  587.8 1.7 fusion.36
  590.5 20.7 %all_to_all.15 = bf16[32,2,2048]{2,1,0:T(2,128)(2,1)} all-to-all(bf16[32,2,2048]{2,1,0:T(2,128)(2,1)S(1)} %reshape.120), channel_id=1, replica_groups=mesh['section'=8,'expert'=32] {'expert'}, dimensions={0} | all-to-all | bytes 524288 | tf_op jit(solution)/shard_map/all_to_all | solution.py:95
  611.5 24.6 %all-gather.5.cloned.1.call-done = bf16[256,2,2048]{2,1,0:T(2,128)(2,1)} async-done(((bf16[32,2,2048]{2,1,0:T(2,128)(2,1)}), bf16[256,2,2048]{2,1,0:T(2,128)(2,1)}) %all-gather.5.cloned.1.call-update) | async-done | bytes 2097168 | tf_op jit(solution)/shard_map/all_gather | solution.py:96
  636.0 2.7 reshape.121
  640.2 4.9 multiply_convert_fusion.2
  645.2 36.3 %reduce-scatter.2.cloned.1.call-done = bf16[512,256]{1,0:T(8,128)(2,1)} async-done(((bf16[512,2048]{1,0:T(8,128)(2,1)}), bf16[512,256]{1,0:T(8,128)(2,1)}) %reduce-scatter.2.cloned.1.call-update) | async-done | bytes 262160 | tf_op jit(solution)/shard_map/reduce_scatter | solution.py:107
  683.4 9.3 %all-to-all-start.2 = ((bf16[32,8,2,256]{3,2,1,0:T(2,128)(2,1)}), bf16[32,8,2,256]{3,2,1,0:T(2,128)(2,1)S(1)}, u32[]{:S(2)}, u32[]{:S(2)}) async-start(bf16[32,8,2,256]{3,2,1,0:T(2,128)(2,1)} %bitcast.86), calls=%async_computation.3 | async-start | bytes 524288 | tf_op jit(solution)/shard_map/all_to_all | solution.py:109
  692.9 12.6 %all-to-all-done.2 = bf16[32,8,2,256]{3,2,1,0:T(2,128)(2,1)S(1)} async-done(((bf16[32,8,2,256]{3,2,1,0:T(2,128)(2,1)}), bf16[32,8,2,256]{3,2,1,0:T(2,128)(2,1)S(1)}, u32[]{:S(2)}, u32[]{:S(2)}) %all-to-all-start.2) | async-done | bytes 262176 | tf_op jit(solution)/shard_map/all_to_all | solution.py:109
  705.6 2.1 scatter_custom_fusion
  (126 shorter events, 74.9 us)
Async XLA Ops:
  6.5 633.7 %copy-start = (bf16[1,256,2048]{2,1,0:T(8,128)(2,1)S(1)}, bf16[1,256,2048]{2,1,0:T(8,128)(2,1)}, u32[]{:S(2)}) copy-start(bf16[1,256,2048]{2,1,0:T(8,128)(2,1)} %param.17) | copy-start | bytes 3145732
  11.9 12.3 %copy-start.6 = (s32[144,1]{0,1:T(1,128)S(1)}, s32[144,1]{0,1:T(1,128)}, u32[]{:S(2)}) copy-start(s32[144,1]{0,1:T(1,128)} %param.19) | copy-start | bytes 1732
  11.9 13.1 %copy-start.7 = (s32[144]{0:T(256)S(1)}, s32[144]{0:T(256)}, u32[]{:S(2)}) copy-start(s32[144]{0:T(256)} %param.18) | copy-start | bytes 1732
  11.9 242.3 %all-to-all-start = ((bf16[32,1,64,2048]{3,2,1,0:T(8,128)(2,1)}), bf16[32,1,64,2048]{3,2,1,0:T(8,128)(2,1)}, u32[]{:S(2)}, u32[]{:S(2)}) async-start(bf16[32,1,64,2048]{3,2,1,0:T(8,128)(2,1)} %stack.2), calls=%async_computation | async-start | bytes 16777216 | tf_op jit(solution)/shard_map/all_to_all | solution.py:37
  23.4 230.8 %all-gather.3.cloned.1.call-start = ((), (), s32[]{:S(2)}) async-start(), calls=%async_computation.4 | async-start | bytes 8650752 | tf_op jit(solution)/shard_map/all_gather | solution.py:35
  24.1 611.9 %all-gather.5.cloned.1.call-start = ((), (), s32[]{:S(2)}) async-start(), calls=%async_computation.5 | async-start | bytes 2359296 | tf_op jit(solution)/shard_map/all_gather | solution.py:96
  256.7 5.4 collective-permute-start
  263.6 8.3 %collective-permute-start = (bf16[72,2048]{1,0:T(8,128)(2,1)}, bf16[72,2048]{1,0:T(8,128)(2,1)}, u32[]{:S(2)}, u32[]{:S(2)}) collective-permute-start(bf16[72,2048]{1,0:T(8,128)(2,1)} %get-tuple-element.294), channel_id=1, source_target_pairs={{0,32},{32,64},{64,96},{96,128},{128,160},{160,192},{192,224},{1,3... | collective-permute-start | bytes 884744 | tf_op jit(solution)/shard_map/while/body/eval_jaxpr/ppermute | solution.py:10
  273.4 8.3 %collective-permute-start = (bf16[72,2048]{1,0:T(8,128)(2,1)}, bf16[72,2048]{1,0:T(8,128)(2,1)}, u32[]{:S(2)}, u32[]{:S(2)}) collective-permute-start(bf16[72,2048]{1,0:T(8,128)(2,1)} %get-tuple-element.294), channel_id=1, source_target_pairs={{0,32},{32,64},{64,96},{96,128},{128,160},{160,192},{192,224},{1,3... | collective-permute-start | bytes 884744 | tf_op jit(solution)/shard_map/while/body/eval_jaxpr/ppermute | solution.py:10
  283.2 8.3 %collective-permute-start = (bf16[72,2048]{1,0:T(8,128)(2,1)}, bf16[72,2048]{1,0:T(8,128)(2,1)}, u32[]{:S(2)}, u32[]{:S(2)}) collective-permute-start(bf16[72,2048]{1,0:T(8,128)(2,1)} %get-tuple-element.294), channel_id=1, source_target_pairs={{0,32},{32,64},{64,96},{96,128},{128,160},{160,192},{192,224},{1,3... | collective-permute-start | bytes 884744 | tf_op jit(solution)/shard_map/while/body/eval_jaxpr/ppermute | solution.py:10
  293.1 8.3 %collective-permute-start = (bf16[72,2048]{1,0:T(8,128)(2,1)}, bf16[72,2048]{1,0:T(8,128)(2,1)}, u32[]{:S(2)}, u32[]{:S(2)}) collective-permute-start(bf16[72,2048]{1,0:T(8,128)(2,1)} %get-tuple-element.294), channel_id=1, source_target_pairs={{0,32},{32,64},{64,96},{96,128},{128,160},{160,192},{192,224},{1,3... | collective-permute-start | bytes 884744 | tf_op jit(solution)/shard_map/while/body/eval_jaxpr/ppermute | solution.py:10
  302.9 8.3 %collective-permute-start = (bf16[72,2048]{1,0:T(8,128)(2,1)}, bf16[72,2048]{1,0:T(8,128)(2,1)}, u32[]{:S(2)}, u32[]{:S(2)}) collective-permute-start(bf16[72,2048]{1,0:T(8,128)(2,1)} %get-tuple-element.294), channel_id=1, source_target_pairs={{0,32},{32,64},{64,96},{96,128},{128,160},{160,192},{192,224},{1,3... | collective-permute-start | bytes 884744 | tf_op jit(solution)/shard_map/while/body/eval_jaxpr/ppermute | solution.py:10
  312.7 68.8 %collective-permute-start = (bf16[72,2048]{1,0:T(8,128)(2,1)}, bf16[72,2048]{1,0:T(8,128)(2,1)}, u32[]{:S(2)}, u32[]{:S(2)}) collective-permute-start(bf16[72,2048]{1,0:T(8,128)(2,1)} %get-tuple-element.294), channel_id=1, source_target_pairs={{0,32},{32,64},{64,96},{96,128},{128,160},{160,192},{192,224},{1,3... | collective-permute-start | bytes 884744 | tf_op jit(solution)/shard_map/while/body/eval_jaxpr/ppermute | solution.py:10
  394.3 8.4 %collective-permute-start = (bf16[72,2048]{1,0:T(8,128)(2,1)}, bf16[72,2048]{1,0:T(8,128)(2,1)}, u32[]{:S(2)}, u32[]{:S(2)}) collective-permute-start(bf16[72,2048]{1,0:T(8,128)(2,1)} %get-tuple-element.294), channel_id=1, source_target_pairs={{0,32},{32,64},{64,96},{96,128},{128,160},{160,192},{192,224},{1,3... | collective-permute-start | bytes 884744 | tf_op jit(solution)/shard_map/while/body/eval_jaxpr/ppermute | solution.py:10
  415.5 8.3 %collective-permute-start = (bf16[72,2048]{1,0:T(8,128)(2,1)}, bf16[72,2048]{1,0:T(8,128)(2,1)}, u32[]{:S(2)}, u32[]{:S(2)}) collective-permute-start(bf16[72,2048]{1,0:T(8,128)(2,1)} %get-tuple-element.294), channel_id=1, source_target_pairs={{0,32},{32,64},{64,96},{96,128},{128,160},{160,192},{192,224},{1,3... | collective-permute-start | bytes 884744 | tf_op jit(solution)/shard_map/while/body/eval_jaxpr/ppermute | solution.py:10
  436.6 8.3 %collective-permute-start = (bf16[72,2048]{1,0:T(8,128)(2,1)}, bf16[72,2048]{1,0:T(8,128)(2,1)}, u32[]{:S(2)}, u32[]{:S(2)}) collective-permute-start(bf16[72,2048]{1,0:T(8,128)(2,1)} %get-tuple-element.294), channel_id=1, source_target_pairs={{0,32},{32,64},{64,96},{96,128},{128,160},{160,192},{192,224},{1,3... | collective-permute-start | bytes 884744 | tf_op jit(solution)/shard_map/while/body/eval_jaxpr/ppermute | solution.py:10
  457.8 8.3 %collective-permute-start = (bf16[72,2048]{1,0:T(8,128)(2,1)}, bf16[72,2048]{1,0:T(8,128)(2,1)}, u32[]{:S(2)}, u32[]{:S(2)}) collective-permute-start(bf16[72,2048]{1,0:T(8,128)(2,1)} %get-tuple-element.294), channel_id=1, source_target_pairs={{0,32},{32,64},{64,96},{96,128},{128,160},{160,192},{192,224},{1,3... | collective-permute-start | bytes 884744 | tf_op jit(solution)/shard_map/while/body/eval_jaxpr/ppermute | solution.py:10
  478.9 8.3 %collective-permute-start = (bf16[72,2048]{1,0:T(8,128)(2,1)}, bf16[72,2048]{1,0:T(8,128)(2,1)}, u32[]{:S(2)}, u32[]{:S(2)}) collective-permute-start(bf16[72,2048]{1,0:T(8,128)(2,1)} %get-tuple-element.294), channel_id=1, source_target_pairs={{0,32},{32,64},{64,96},{96,128},{128,160},{160,192},{192,224},{1,3... | collective-permute-start | bytes 884744 | tf_op jit(solution)/shard_map/while/body/eval_jaxpr/ppermute | solution.py:10
  500.1 8.3 %collective-permute-start = (bf16[72,2048]{1,0:T(8,128)(2,1)}, bf16[72,2048]{1,0:T(8,128)(2,1)}, u32[]{:S(2)}, u32[]{:S(2)}) collective-permute-start(bf16[72,2048]{1,0:T(8,128)(2,1)} %get-tuple-element.294), channel_id=1, source_target_pairs={{0,32},{32,64},{64,96},{96,128},{128,160},{160,192},{192,224},{1,3... | collective-permute-start | bytes 884744 | tf_op jit(solution)/shard_map/while/body/eval_jaxpr/ppermute | solution.py:10
  521.3 8.3 %collective-permute-start = (bf16[72,2048]{1,0:T(8,128)(2,1)}, bf16[72,2048]{1,0:T(8,128)(2,1)}, u32[]{:S(2)}, u32[]{:S(2)}) collective-permute-start(bf16[72,2048]{1,0:T(8,128)(2,1)} %get-tuple-element.294), channel_id=1, source_target_pairs={{0,32},{32,64},{64,96},{96,128},{128,160},{160,192},{192,224},{1,3... | collective-permute-start | bytes 884744 | tf_op jit(solution)/shard_map/while/body/eval_jaxpr/ppermute | solution.py:10
  542.4 3.8 collective-permute-start
  557.7 2.3 copy-start.1
  559.9 9.7 %collective-permute-start.1 = (bf16[136,2048]{1,0:T(8,128)(2,1)S(1)}, bf16[136,2048]{1,0:T(8,128)(2,1)S(1)}, u32[]{:S(2)}, u32[]{:S(2)}) collective-permute-start(bf16[136,2048]{1,0:T(8,128)(2,1)S(1)} %get-tuple-element.231), channel_id=1, source_target_pairs={{224,192},{225,193},{226,194},{227,195},{228,196},{229,197},{230,1... | collective-permute-start | bytes 1671176 | tf_op jit(solution)/shard_map/ppermute | solution.py:90
  562.0 9.7 %collective-permute-start.2 = (bf16[136,2048]{1,0:T(8,128)(2,1)S(1)}, bf16[136,2048]{1,0:T(8,128)(2,1)S(1)}, u32[]{:S(2)}, u32[]{:S(2)}) collective-permute-start(bf16[136,2048]{1,0:T(8,128)(2,1)S(1)} %get-tuple-element.232), channel_id=1, source_target_pairs={{224,160},{225,161},{226,162},{227,163},{228,164},{229,165},{230,1... | collective-permute-start | bytes 1671176 | tf_op jit(solution)/shard_map/ppermute | solution.py:90
  563.3 12.5 %collective-permute-start.3 = (bf16[136,2048]{1,0:T(8,128)(2,1)}, bf16[136,2048]{1,0:T(8,128)(2,1)}, u32[]{:S(2)}, u32[]{:S(2)}) collective-permute-start(bf16[136,2048]{1,0:T(8,128)(2,1)} %get-tuple-element.233), channel_id=1, source_target_pairs={{224,128},{225,129},{226,130},{227,131},{228,132},{229,133},{230,1... | collective-permute-start | bytes 1671176 | tf_op jit(solution)/shard_map/ppermute | solution.py:90
  565.4 16.3 %collective-permute-start.4 = (bf16[136,2048]{1,0:T(8,128)(2,1)}, bf16[136,2048]{1,0:T(8,128)(2,1)}, u32[]{:S(2)}, u32[]{:S(2)}) collective-permute-start(bf16[136,2048]{1,0:T(8,128)(2,1)} %get-tuple-element.234), channel_id=1, source_target_pairs={{224,96},{225,97},{226,98},{227,99},{228,100},{229,101},{230,102},... | collective-permute-start | bytes 1671176 | tf_op jit(solution)/shard_map/ppermute | solution.py:90
  567.5 20.2 %collective-permute-start.5 = (bf16[136,2048]{1,0:T(8,128)(2,1)}, bf16[136,2048]{1,0:T(8,128)(2,1)}, u32[]{:S(2)}, u32[]{:S(2)}) collective-permute-start(bf16[136,2048]{1,0:T(8,128)(2,1)} %get-tuple-element.235), channel_id=1, source_target_pairs={{224,64},{225,65},{226,66},{227,67},{228,68},{229,69},{230,70},{23... | collective-permute-start | bytes 1671176 | tf_op jit(solution)/shard_map/ppermute | solution.py:90
  569.6 2.1 copy-start.4
  569.6 18.1 %collective-permute-start.6 = (bf16[136,2048]{1,0:T(8,128)(2,1)}, bf16[136,2048]{1,0:T(8,128)(2,1)}, u32[]{:S(2)}, u32[]{:S(2)}) collective-permute-start(bf16[136,2048]{1,0:T(8,128)(2,1)} %get-tuple-element.236), channel_id=1, source_target_pairs={{224,32},{225,33},{226,34},{227,35},{228,36},{229,37},{230,38},{23... | collective-permute-start | bytes 1671176 | tf_op jit(solution)/shard_map/ppermute | solution.py:90
  571.7 0.8 copy-start.5
  572.6 15.2 %collective-permute-start.7 = (bf16[136,2048]{1,0:T(8,128)(2,1)}, bf16[136,2048]{1,0:T(8,128)(2,1)}, u32[]{:S(2)}, u32[]{:S(2)}) collective-permute-start(bf16[136,2048]{1,0:T(8,128)(2,1)} %get-tuple-element.230), channel_id=1, source_target_pairs={{224,0},{225,1},{226,2},{227,3},{228,4},{229,5},{230,6},{231,7},{2... | collective-permute-start | bytes 1671176 | tf_op jit(solution)/shard_map/ppermute | solution.py:90
  589.5 0.8 copy-start.2
  611.2 70.3 %reduce-scatter.2.cloned.1.call-start = ((), (), s32[]{:S(2)}) async-start(), calls=%async_computation.6 | async-start | bytes 2359296 | tf_op jit(solution)/shard_map/reduce_scatter | solution.py:107
  645.1 47.7 %copy-start.3 = (bf16[136,2048]{1,0:T(8,128)(2,1)S(1)}, bf16[136,2048]{1,0:T(8,128)(2,1)}, u32[]{:S(2)}) copy-start(bf16[136,2048]{1,0:T(8,128)(2,1)} %copy-done.2) | copy-start | bytes 1671172
  683.4 22.1 %all-to-all-start.2 = ((bf16[32,8,2,256]{3,2,1,0:T(2,128)(2,1)}), bf16[32,8,2,256]{3,2,1,0:T(2,128)(2,1)S(1)}, u32[]{:S(2)}, u32[]{:S(2)}) async-start(bf16[32,8,2,256]{3,2,1,0:T(2,128)(2,1)} %bitcast.86), calls=%async_computation.3 | async-start | bytes 524288 | tf_op jit(solution)/shard_map/all_to_all | solution.py:109
Sparse Core Ops, SparseCore 0:
  26.7 220.2 all-gather.2
  611.4 24.6 all-gather.4
  645.3 36.1 reduce-scatter.1
